TPU v7x, 512 devices: a whole 4x4x16 slice. The times are simulated.
512 devices in a mesh: patch: 16 (over y, x_hi, core), map: 32 (over x_lo, z).
Axes of the slice: x: 4 (x_hi: 2, x_lo: 2; x = x_hi * 2 + x_lo), y: 4, z: 16, core: 2. Of those that a mesh axis runs over, the one named last changes fastest.
Arguments:
- maps: bfloat16 [64, 32, 24576], P('map', None, 'patch'), may hold values from -6 to 6
- cotangent: bfloat16 [64, 32, 24576], P('map', None, 'patch'), may hold values from -6 to 6
- tiles: bfloat16 [96, 3, 256, 256], P('patch'), may hold values from -0.21875 to 0.21875
- columns: int32 [96, 3], P('patch'), may hold values from 0 to 95, as said below
- filters: bfloat16 [3, 32, 32], replicated, may hold values from -0.625 to 0.625
Outputs:
- output: bfloat16 [64, 32, 24576], P('map', None, 'patch')
- input_grad: bfloat16 [64, 32, 24576], P('map', None, 'patch')
- filter_grad: float32 [3, 32, 32], replicated
Inputs may be any that keep to these rules, and one draw needn't show every extreme that they name: `columns`: slot 0 of block row b names block b itself, slot 1 a block 1 to 2 before it and slot 2 a block 1 to 2 after it, counted cyclically over the 96 blocks; block row 0 reads exactly 2 blocks away on both sides.
All inputs are finite; a program needn't handle non-finite values.
Results may differ from a plain program's by a relative error of at most 0.0054.
Values may be sent and summed in bfloat16 or wider, within the bound.
No kernel may reach another device: no remote copies, remote signals or barrier semaphores. Data moves between devices by JAX's collectives and lax.ppermute only.
A program may use at most 64 MiB of HBM per device.

v0:
```python
import math
import jax
import jax.numpy as jnp
from jax import lax
from jax.sharding import PartitionSpec as P

REACH = 2


def extended_2(cells, sides, width):
    for axis, dim in sides:
        count = lax.axis_size(axis)
        head = lax.slice_in_dim(cells, 0, width, axis=dim)
        tail = lax.slice_in_dim(cells, cells.shape[dim] - width, cells.shape[dim], axis=dim)
        cells = jnp.concatenate(
            [
                lax.ppermute(tail, axis, [(i, (i + 1) % count) for i in range(count)]),
                cells,
                lax.ppermute(head, axis, [((i + 1) % count, i) for i in range(count)]),
            ],
            axis=dim,
        )
    return cells


def offset_sums(grad_blocks, tile_set, offset_mask):
    contrib = jnp.einsum(
        "nui,ujiq->nujq", grad_blocks, tile_set, preferred_element_type=jnp.float32
    )
    return jnp.einsum(
        "uje,nujq->nueq", offset_mask.astype(jnp.float32), contrib, precision=lax.Precision.HIGHEST
    )


def per_device(maps, cotangent, tiles, columns, filters):
    map_count = maps.shape[0]
    chan_count = maps.shape[1]
    pix_count = maps.shape[2]
    block_count = tiles.shape[0]
    block_size = tiles.shape[2]
    reach_blocks = REACH
    spread = 2 * reach_blocks + 1
    row_count = map_count * chan_count
    rim_cells = reach_blocks * block_size
    patch_count = lax.axis_size("patch")
    total_blocks = block_count * patch_count
    first_block = lax.axis_index("patch") * block_count
    row_ids = first_block + jnp.arange(block_count, dtype=jnp.int32)
    offset_ids = jnp.arange(spread, dtype=jnp.int32)
    own_offset = (columns - row_ids[:, None] + reach_blocks) % total_blocks
    own_mask = own_offset[:, :, None] == offset_ids[None, None, :]

    def forward_apply(field):
        extended = extended_2(field, (("patch", 2),), rim_cells)
        ext_blocks = extended.reshape(row_count, block_count + 2 * reach_blocks, block_size)
        shifted = jnp.stack(
            [ext_blocks[:, offset : offset + block_count] for offset in range(spread)], axis=2
        )
        picked = jnp.einsum(
            "rje,nreq->nrjq",
            own_mask.astype(jnp.bfloat16),
            shifted,
            preferred_element_type=jnp.bfloat16,
        )
        result = jnp.einsum("nrjq,rjiq->nri", picked, tiles, preferred_element_type=jnp.float32)
        return result.reshape(map_count, chan_count, pix_count)

    def adjoint_apply(grads):
        by_offset = offset_sums(grads.reshape(row_count, block_count, block_size), tiles, own_mask)
        window = jnp.pad(by_offset[:, :, 0], ((0, 0), (0, spread - 1), (0, 0)))
        for offset in range(1, spread):
            window = window + jnp.pad(
                by_offset[:, :, offset], ((0, 0), (offset, spread - 1 - offset), (0, 0))
            )
        own_part = window[:, reach_blocks : reach_blocks + block_count]
        outgoing = jnp.concatenate(
            [window[:, :reach_blocks], window[:, reach_blocks + block_count :]], axis=1
        )
        outgoing = outgoing.reshape(map_count, chan_count, 2 * rim_cells)
        incoming = extended_2(outgoing, (("patch", 2),), rim_cells)
        from_left = incoming[:, :, :rim_cells].reshape(row_count, reach_blocks, block_size)
        from_right = incoming[:, :, incoming.shape[2] - rim_cells :].reshape(
            row_count, reach_blocks, block_size
        )
        own_part = own_part.at[:, :reach_blocks].add(from_left)
        own_part = own_part.at[:, block_count - reach_blocks :].add(from_right)
        return own_part.reshape(map_count, chan_count, pix_count)

    x_one = forward_apply(maps).astype(jnp.bfloat16)
    x_two = (2.0 * forward_apply(x_one) - maps.astype(jnp.float32)).astype(jnp.bfloat16)
    terms = jnp.stack([maps, x_one, x_two])
    output = jnp.einsum("kco,kmcp->mop", filters, terms, preferred_element_type=jnp.float32).astype(
        jnp.bfloat16
    )
    grads = jnp.einsum("kco,mop->kmcp", filters, cotangent, preferred_element_type=jnp.float32)
    grad_two = grads[2].astype(jnp.bfloat16)
    update = (grads[1] + 2.0 * adjoint_apply(grad_two)).astype(jnp.bfloat16)
    input_grad = (grads[0] - grad_two.astype(jnp.float32) + adjoint_apply(update)).astype(
        jnp.bfloat16
    )
    scale = 1.0 / math.sqrt(map_count * lax.axis_size("map") * pix_count * patch_count)
    local_grad = jnp.einsum("kmcp,mop->kco", terms, cotangent, preferred_element_type=jnp.float32)
    filter_grad = lax.psum(local_grad, ("patch", "map")) * scale
    return (output, input_grad, filter_grad)


def solution(mesh):
    placed = (
        P("map", None, "patch"),
        P("map", None, "patch"),
        P("patch", None, None, None),
        P("patch", None),
        P(),
    )
    return jax.shard_map(
        per_device,
        mesh=mesh,
        in_specs=placed,
        out_specs=(P("map", None, "patch"), P("map", None, "patch"), P()),
        check_vma=False,
    )
```

profile of v0, /device:TPU:1, one launch (start us, length us, event | category | flops | bytes accessed | tf_op | source)
XLA Modules:
  0.0 221.6 jit_solution(9846326644404595408)
XLA Ops:
  4.6 2.3 %convolution_bitcast_fusion.3 = f32[64,6,5,256]{3,2,0,1:T(8,128)S(1)} fusion(f32[6,64,3,256]{3,1,2,0:T(8,128)S(1)} %fusion.38, s32[6,3]{1,0:T(8,128)S(1)} %copy.21), kind=kOutput, calls=%fused_computation.5 | convolution fusion | flops 17694810 | bytes 3145800 | tf_op jit(solution)/shard_map/uje,nujq->nueq/dot_general | solution.py:30
  6.9 1.8 fusion.56
  10.8 1.8 reshape.181
  12.6 1.8 fusion.58
  14.4 6.0 %collective-permute-start.4 = (f32[2,32,512]{2,1,0:T(8,128)}, f32[2,32,512]{2,1,0:T(8,128)}, u32[]{:S(2)}, u32[]{:S(2)}) collective-permute-start(f32[2,32,512]{2,1,0:T(8,128)} %get-tuple-element.68), channel_id=1, source_target_pairs={{0,32},{32,64},{64,96},{96,128},{128,160},{160,192},{192,224},{224... | collective-permute-start | bytes 393224 | tf_op jit(solution)/shard_map/ppermute | solution.py:17
  20.4 4.7 %collective-permute-start.5 = (f32[2,32,512]{2,1,0:T(8,128)}, f32[2,32,512]{2,1,0:T(8,128)}, u32[]{:S(2)}, u32[]{:S(2)}) collective-permute-start(f32[2,32,512]{2,1,0:T(8,128)} %get-tuple-element.67), channel_id=1, source_target_pairs={{32,0},{64,32},{96,64},{128,96},{160,128},{192,160},{224,192},{256... | collective-permute-start | bytes 393224 | tf_op jit(solution)/shard_map/ppermute | solution.py:19
  26.6 2.4 %collective-permute-start = (bf16[2,32,512]{2,1,0:T(8,128)(2,1)}, bf16[2,32,512]{2,1,0:T(8,128)(2,1)}, u32[]{:S(2)}, u32[]{:S(2)}) collective-permute-start(bf16[2,32,512]{2,1,0:T(8,128)(2,1)} %get-tuple-element.71), channel_id=1, source_target_pairs={{0,32},{32,64},{64,96},{96,128},{128,160},{160,192},{192,224},{224... | collective-permute-start | bytes 196616 | tf_op jit(solution)/shard_map/ppermute | solution.py:17
  29.0 6.8 %collective-permute-start.1 = (bf16[2,32,512]{2,1,0:T(8,128)(2,1)}, bf16[2,32,512]{2,1,0:T(8,128)(2,1)}, u32[]{:S(2)}, u32[]{:S(2)}) collective-permute-start(bf16[2,32,512]{2,1,0:T(8,128)(2,1)} %get-tuple-element.72), channel_id=1, source_target_pairs={{32,0},{64,32},{96,64},{128,96},{160,128},{192,160},{224,192},{256... | collective-permute-start | bytes 196616 | tf_op jit(solution)/shard_map/ppermute | solution.py:19
  35.8 1.8 slice.264
  38.5 1.9 squeeze.35
  46.6 1.9 convert_element_type.73
  48.4 1.9 convert_element_type.72
  51.8 1.9 collective-permute-start.2
  53.7 7.4 %collective-permute-start.3 = (bf16[2,32,512]{2,1,0:T(8,128)(2,1)}, bf16[2,32,512]{2,1,0:T(8,128)(2,1)}, u32[]{:S(2)}, u32[]{:S(2)}) collective-permute-start(bf16[2,32,512]{2,1,0:T(8,128)(2,1)} %get-tuple-element.70), channel_id=1, source_target_pairs={{32,0},{64,32},{96,64},{128,96},{160,128},{192,160},{224,192},{256... | collective-permute-start | bytes 196616 | tf_op jit(solution)/shard_map/ppermute | solution.py:19
  68.7 2.3 %convolution_bitcast_fusion.2 = f32[64,6,5,256]{3,2,0,1:T(8,128)S(1)} fusion(f32[6,64,3,256]{3,1,2,0:T(8,128)S(1)} %fusion.34, s32[6,3]{1,0:T(8,128)S(1)} %copy.21), kind=kOutput, calls=%fused_computation.4 | convolution fusion | flops 17694810 | bytes 3145800 | tf_op jit(solution)/shard_map/uje,nujq->nueq/dot_general | solution.py:30
  71.0 1.8 fusion.55
  82.8 2.0 convolution_bitcast_fusion.6
  86.7 1.8 reshape.184
  90.1 1.9 collective-permute-start.6
  92.0 1.8 slice.279
  93.8 7.2 %collective-permute-start.7 = (f32[2,32,512]{2,1,0:T(8,128)}, f32[2,32,512]{2,1,0:T(8,128)}, u32[]{:S(2)}, u32[]{:S(2)}) collective-permute-start(f32[2,32,512]{2,1,0:T(8,128)} %get-tuple-element.65), channel_id=1, source_target_pairs={{32,0},{64,32},{96,64},{128,96},{160,128},{192,160},{224,192},{256... | collective-permute-start | bytes 393224 | tf_op jit(solution)/shard_map/ppermute | solution.py:19
  101.0 106.8 %psum.7 = f32[3,32,32]{2,1,0:T(8,128)} all-reduce(f32[3,32,32]{2,1,0:T(8,128)} %convolution_bitcast_fusion.6), channel_id=1, replica_groups=mesh['patch'=16,'map'=32] {'patch','map'}, use_global_device_ids=true, to_apply=%region_0.1 | all-reduce | flops 3072 | bytes 24576 | tf_op jit(solution)/shard_map/psum | solution.py:103
  215.9 2.0 copy.42
  218.0 1.9 reshape.187
  (117 shorter events, 46.7 us)
Async XLA Ops:
  0.6 3.5 %copy-start = (bf16[6,3,256,256]{3,2,1,0:T(8,128)(2,1)S(1)}, bf16[6,3,256,256]{3,2,1,0:T(8,128)(2,1)}, u32[]{:S(2)}) copy-start(bf16[6,3,256,256]{3,2,1,0:T(8,128)(2,1)} %param.15) | copy-start | bytes 7077892
  8.9 28.7 %copy-start.7 = (f32[64,6,256]{2,0,1:T(8,128)}, f32[64,6,256]{2,0,1:T(8,128)S(1)}, u32[]{:S(2)}) copy-start(f32[64,6,256]{2,0,1:T(8,128)S(1)} %get-tuple-element.73) | copy-start | bytes 1179652
  8.9 28.7 %copy-start.9 = (f32[64,6,256]{2,0,1:T(8,128)}, f32[64,6,256]{2,0,1:T(8,128)S(1)}, u32[]{:S(2)}) copy-start(f32[64,6,256]{2,0,1:T(8,128)S(1)} %get-tuple-element.74) | copy-start | bytes 1179652
  12.6 25.0 %copy-start.12 = (f32[64,6,256]{2,0,1:T(8,128)S(1)}, f32[64,6,256]{2,0,1:T(8,128)}, u32[]{:S(2)}) copy-start(f32[64,6,256]{2,0,1:T(8,128)} %copy-done.11) | copy-start | bytes 1179652
  12.6 25.0 %copy-start.14 = (f32[64,6,256]{2,0,1:T(8,128)S(1)}, f32[64,6,256]{2,0,1:T(8,128)}, u32[]{:S(2)}) copy-start(f32[64,6,256]{2,0,1:T(8,128)} %copy-done.13) | copy-start | bytes 1179652
  14.4 46.8 %collective-permute-start.4 = (f32[2,32,512]{2,1,0:T(8,128)}, f32[2,32,512]{2,1,0:T(8,128)}, u32[]{:S(2)}, u32[]{:S(2)}) collective-permute-start(f32[2,32,512]{2,1,0:T(8,128)} %get-tuple-element.68), channel_id=1, source_target_pairs={{0,32},{32,64},{64,96},{96,128},{128,160},{160,192},{192,224},{224... | collective-permute-start | bytes 393224 | tf_op jit(solution)/shard_map/ppermute | solution.py:17
  20.4 44.1 %collective-permute-start.5 = (f32[2,32,512]{2,1,0:T(8,128)}, f32[2,32,512]{2,1,0:T(8,128)}, u32[]{:S(2)}, u32[]{:S(2)}) collective-permute-start(f32[2,32,512]{2,1,0:T(8,128)} %get-tuple-element.67), channel_id=1, source_target_pairs={{32,0},{64,32},{96,64},{128,96},{160,128},{192,160},{224,192},{256... | collective-permute-start | bytes 393224 | tf_op jit(solution)/shard_map/ppermute | solution.py:19
  26.6 13.8 %collective-permute-start = (bf16[2,32,512]{2,1,0:T(8,128)(2,1)}, bf16[2,32,512]{2,1,0:T(8,128)(2,1)}, u32[]{:S(2)}, u32[]{:S(2)}) collective-permute-start(bf16[2,32,512]{2,1,0:T(8,128)(2,1)} %get-tuple-element.71), channel_id=1, source_target_pairs={{0,32},{32,64},{64,96},{96,128},{128,160},{160,192},{192,224},{224... | collective-permute-start | bytes 196616 | tf_op jit(solution)/shard_map/ppermute | solution.py:17
  29.0 11.4 %collective-permute-start.1 = (bf16[2,32,512]{2,1,0:T(8,128)(2,1)}, bf16[2,32,512]{2,1,0:T(8,128)(2,1)}, u32[]{:S(2)}, u32[]{:S(2)}) collective-permute-start(bf16[2,32,512]{2,1,0:T(8,128)(2,1)} %get-tuple-element.72), channel_id=1, source_target_pairs={{32,0},{64,32},{96,64},{128,96},{160,128},{192,160},{224,192},{256... | collective-permute-start | bytes 196616 | tf_op jit(solution)/shard_map/ppermute | solution.py:19
  37.7 2.7 %copy-start.18 = (bf16[2,32,1536]{2,1,0:T(8,128)(2,1)S(1)}, bf16[2,32,1536]{2,1,0:T(8,128)(2,1)}, u32[]{:S(2)}) copy-start(bf16[2,32,1536]{2,1,0:T(8,128)(2,1)} %param.13) | copy-start | bytes 589828
  45.7 17.1 %copy-start.8 = (f32[64,6,256]{2,0,1:T(8,128)S(1)}, f32[64,6,256]{2,0,1:T(8,128)}, u32[]{:S(2)}) copy-start(f32[64,6,256]{2,0,1:T(8,128)} %copy-done.7) | copy-start | bytes 1179652
  45.7 17.1 %copy-start.10 = (f32[64,6,256]{2,0,1:T(8,128)S(1)}, f32[64,6,256]{2,0,1:T(8,128)}, u32[]{:S(2)}) copy-start(f32[64,6,256]{2,0,1:T(8,128)} %copy-done.9) | copy-start | bytes 1179652
  51.8 23.2 %collective-permute-start.2 = (bf16[2,32,512]{2,1,0:T(8,128)(2,1)}, bf16[2,32,512]{2,1,0:T(8,128)(2,1)}, u32[]{:S(2)}, u32[]{:S(2)}) collective-permute-start(bf16[2,32,512]{2,1,0:T(8,128)(2,1)} %get-tuple-element.69), channel_id=1, source_target_pairs={{0,32},{32,64},{64,96},{96,128},{128,160},{160,192},{192,224},{224... | collective-permute-start | bytes 196616 | tf_op jit(solution)/shard_map/ppermute | solution.py:17
  53.7 21.3 %collective-permute-start.3 = (bf16[2,32,512]{2,1,0:T(8,128)(2,1)}, bf16[2,32,512]{2,1,0:T(8,128)(2,1)}, u32[]{:S(2)}, u32[]{:S(2)}) collective-permute-start(bf16[2,32,512]{2,1,0:T(8,128)(2,1)} %get-tuple-element.70), channel_id=1, source_target_pairs={{32,0},{64,32},{96,64},{128,96},{160,128},{192,160},{224,192},{256... | collective-permute-start | bytes 196616 | tf_op jit(solution)/shard_map/ppermute | solution.py:19
  72.9 1.3 copy-start.1
  81.7 3.1 %copy-start.22 = (bf16[1,2,32,1536]{3,2,1,0:T(8,128)(2,1)S(1)}, bf16[1,2,32,1536]{3,2,1,0:T(8,128)(2,1)}, u32[]{:S(2)}) copy-start(bf16[1,2,32,1536]{3,2,1,0:T(8,128)(2,1)} %convert_element_type.72) | copy-start | bytes 589828
  81.7 3.1 %copy-start.23 = (bf16[3,32,32]{2,1,0:T(8,128)(2,1)S(1)}, bf16[3,32,32]{2,1,0:T(8,128)(2,1)}, u32[]{:S(2)}) copy-start(bf16[3,32,32]{2,1,0:T(8,128)(2,1)} %param.17) | copy-start | bytes 18436
  82.8 3.0 %copy-start.20 = (f32[64,2,256]{2,0,1:T(8,128)S(1)}, f32[64,2,256]{2,0,1:T(8,128)}, u32[]{:S(2)}) copy-start(f32[64,2,256]{2,0,1:T(8,128)} %get-tuple-element.61) | copy-start | bytes 393220
  82.8 3.0 %copy-start.21 = (f32[64,2,256]{2,0,1:T(8,128)S(1)}, f32[64,2,256]{2,0,1:T(8,128)}, u32[]{:S(2)}) copy-start(f32[64,2,256]{2,0,1:T(8,128)} %get-tuple-element.62) | copy-start | bytes 393220
  85.8 125.1 %copy-start.2 = (f32[64,6,1,256]{3,0,1,2:T(8,128)S(1)}, f32[64,6,1,256]{3,0,1,2:T(8,128)}, u32[]{:S(2)}) copy-start(f32[64,6,1,256]{3,0,1,2:T(8,128)} %copy-done.1) | copy-start | bytes 1179652
  85.8 125.1 %copy-start.4 = (f32[64,6,1,256]{3,0,1,2:T(8,128)S(1)}, f32[64,6,1,256]{3,0,1,2:T(8,128)}, u32[]{:S(2)}) copy-start(f32[64,6,1,256]{3,0,1,2:T(8,128)} %copy-done.3) | copy-start | bytes 1179652
  90.1 119.1 %collective-permute-start.6 = (f32[2,32,512]{2,1,0:T(8,128)}, f32[2,32,512]{2,1,0:T(8,128)}, u32[]{:S(2)}, u32[]{:S(2)}) collective-permute-start(f32[2,32,512]{2,1,0:T(8,128)} %get-tuple-element.66), channel_id=1, source_target_pairs={{0,32},{32,64},{64,96},{96,128},{128,160},{160,192},{192,224},{224... | collective-permute-start | bytes 393224 | tf_op jit(solution)/shard_map/ppermute | solution.py:17
  93.8 118.8 %collective-permute-start.7 = (f32[2,32,512]{2,1,0:T(8,128)}, f32[2,32,512]{2,1,0:T(8,128)}, u32[]{:S(2)}, u32[]{:S(2)}) collective-permute-start(f32[2,32,512]{2,1,0:T(8,128)} %get-tuple-element.65), channel_id=1, source_target_pairs={{32,0},{64,32},{96,64},{128,96},{160,128},{192,160},{224,192},{256... | collective-permute-start | bytes 393224 | tf_op jit(solution)/shard_map/ppermute | solution.py:19
  212.5 7.3 %copy-start.16 = (f32[3,2,32,1536]{3,2,0,1:T(8,128)S(1)}, f32[3,2,32,1536]{3,2,0,1:T(8,128)}, u32[]{:S(2)}) copy-start(f32[3,2,32,1536]{3,2,0,1:T(8,128)} %copy-done.15) | copy-start | bytes 3538948
  (8 other events, 8.8 us)
where the time goes:
time: 223 us; the launch traced here: 222 us
  blocking collectives  107 us (48%)
  local copies, waits for them, and re-layouts  43.2 us (19%)
  starting transfers between devices  38.4 us (17%)
  other arithmetic  17 us (8%)
  matrix products  15.1 us (7%)
    psum x1, blocking collectives, per_device(): filter_grad = lax.psum(local_grad, ('patch', 'map')) * scale  107 us
    ppermute x4, starting transfers between devices, extended_2(): lax.ppermute(head, axis, [((i + 1) % count, i) for i in range(count)])  26.1 us
    ppermute x4, starting transfers between devices, extended_2(): lax.ppermute(tail, axis, [(i, (i + 1) % count) for i in range(count)])  12.2 us
    another operation x4, local copies, waits for them, and re-layouts  6 us
    dot_general x2, matrix products, offset_sums(): jnp.einsum('uje,nujq->nueq', offset_mask.astype(jnp.float32), contrib, pr...  4.57 us
    convert_element_type x3, local copies, waits for them, and re-layouts, per_device(): x_one = forward_apply(maps).astype(jnp.bfloat16)  4.53 us
  transfers between devices with their start and end apart: 8, of which 0 were waited for; matrix products, arithmetic and copies ran while one was open for 17% of the time, Pallas kernels for 0%

commit v1 on v0

--- a/solution.py
+++ b/solution.py
@@ -100,7 +100,7 @@
     )
     scale = 1.0 / math.sqrt(map_count * lax.axis_size("map") * pix_count * patch_count)
     local_grad = jnp.einsum("kmcp,mop->kco", terms, cotangent, preferred_element_type=jnp.float32)
-    filter_grad = lax.psum(local_grad, ("patch", "map")) * scale
+    filter_grad = jnp.sum(lax.all_gather(local_grad, ("patch", "map")), axis=0) * scale
     return (output, input_grad, filter_grad)
 
 

time: 223 us -> 1550 us (6.95)
  waiting for transfers between devices: 0.02 us -> 1400 us
  blocking collectives: 107 us -> 0 us
    all_gather x0 -> x1, waiting for transfers between devices: none -> 1400 us  [per_device(): lax.all_gather(local_grad, ('patch', 'map'))]
    psum x1 -> x0, blocking collectives: 107 us -> none  [per_device(): filter_grad = lax.psum(local_grad, ('patch', 'map')) * scale]
    another operation x2 -> x14, local copies, waits for them, and re-layouts: 0.16 us -> 21.9 us  [forward_apply(): jnp.stack([ext_blocks[:, offset:offset + block_count] for offset in range...]
  transfers between devices with their start and end apart: 8 -> 9, of which waited for: 0 -> 3; matrix products, arithmetic and copies ran while one was open for 17% -> 2% of each run, Pallas kernels for 0% -> 0%
where the time goes in v1:
time: 1550 us; the launch traced here: 1540 us
  waiting for transfers between devices  1400 us (90%)
  local copies, waits for them, and re-layouts  46.2 us (3%)
  starting transfers between devices  40.1 us (3%)
  other arithmetic  18.2 us (1%)
    all_gather x1, waiting for transfers between devices, per_device(): lax.all_gather(local_grad, ('patch', 'map'))  1400 us
  transfers between devices with their start and end apart: 9, of which 3 were waited for; matrix products, arithmetic and copies ran while one was open for 2% of the time, Pallas kernels for 0%

profile of v1, /device:TPU:1, one launch (start us, length us, event | category | flops | bytes accessed | tf_op | source)
XLA Modules:
  0.0 1539.1 jit_solution(73321943337752686)
XLA Ops:
  8.3 6.0 collective-permute-start
  14.3 4.7 collective-permute-start.1
  25.8 7.7 stack.52
  33.5 2.0 convolution_bitcast_fusion.7
  36.8 1.9 collective-permute-start.2
  38.7 6.9 collective-permute-start.3
  50.1 7.7 stack.58
  57.8 2.0 convolution_bitcast_fusion.6
  62.3 1.9 convolution_bitcast_fusion.10
  66.3 2.3 convolution_bitcast_fusion.3
  68.6 1.8 fusion.36
  72.4 1.8 reshape.181
  75.9 8.1 collective-permute-start.5
  84.0 2.1 collective-permute-start.4
  86.2 1.8 slice.264
  88.0 1.9 squeeze.35
  95.2 1.8 fusion.24
  100.0 2.3 convolution_bitcast_fusion.2
  102.3 1.8 fusion.35
  104.7 8.3 collective-permute-start.7
  113.0 2.1 collective-permute-start.6
  116.3 3.9 collective-permute-done.6
  122.4 1398.9 %all-gather.3.cloned.1.call-done = f32[1536,32,32]{2,1,0:T(8,128)} async-done(((f32[3,32,32]{2,1,0:T(8,128)}), f32[1536,32,32]{2,1,0:T(8,128)}) %all-gather.3.cloned.1.call-update) | async-done | bytes 6291472 | tf_op jit(solution)/shard_map/all_gather | solution.py:103
  1521.4 10.3 reduce_sum.9
  (108 shorter events, 34.4 us)
Async XLA Ops:
  7.2 28.4 %copy-start = (bf16[6,3,256,256]{3,2,1,0:T(8,128)(2,1)S(1)}, bf16[6,3,256,256]{3,2,1,0:T(8,128)(2,1)}, u32[]{:S(2)}) copy-start(bf16[6,3,256,256]{3,2,1,0:T(8,128)(2,1)} %param.15) | copy-start | bytes 7077892
  7.2 1514.2 %all-gather.3.cloned.1.call-start = ((), (), s32[]{:S(2)}) async-start(), calls=%async_computation | async-start | bytes 25214976 | tf_op jit(solution)/shard_map/all_gather | solution.py:103
  8.3 11.5 collective-permute-start
  14.3 7.1 collective-permute-start.1
  36.8 9.8 collective-permute-start.2
  38.7 7.8 collective-permute-start.3
  60.6 0.9 copy-start.7
  61.6 2.7 copy-start.13
  61.6 2.7 copy-start.14
  64.6 1.0 copy-start.4
  70.6 0.8 copy-start.2
  70.6 0.9 copy-start.3
  75.9 16.0 %collective-permute-start.5 = (f32[2,32,512]{2,1,0:T(8,128)}, f32[2,32,512]{2,1,0:T(8,128)}, u32[]{:S(2)}, u32[]{:S(2)}) collective-permute-start(f32[2,32,512]{2,1,0:T(8,128)} %get-tuple-element.77), channel_id=1, source_target_pairs={{32,0},{64,32},{96,64},{128,96},{160,128},{192,160},{224,192},{256... | collective-permute-start | bytes 393224 | tf_op jit(solution)/shard_map/ppermute | solution.py:19
  84.0 9.5 collective-permute-start.4
  95.2 1.8 copy-start.9
  95.2 3.3 copy-start.6
  104.7 11.6 collective-permute-start.7
  113.0 2.3 copy-start.8
  113.0 2.3 copy-start.10
  113.0 2.3 copy-start.12
  113.0 2.3 copy-start.15
  113.0 7.3 collective-permute-start.6
  120.4 1.3 copy-start.5
  1521.4 10.9 copy-start.1
  (1 other events, 0.7 us)
Sparse Core Ops, SparseCore 0:
  64.4 1456.9 all-gather.2
